TPU v7x, 128 devices: a whole 4x4x4 slice. The times are simulated.
128 devices in a mesh: wave: 8 (over z_lo, x), strip: 16 (over y, z_hi, core).
Axes of the slice: x: 4, y: 4, z: 4 (z_hi: 2, z_lo: 2; z = z_hi * 2 + z_lo), core: 2. Of those that a mesh axis runs over, the one named last changes fastest.
Arguments:
- unit_params: float32 [9, 16, 24576], P(None, 'strip', 'wave'), may hold values from 0 to 1
- observed: bfloat16 [4, 256, 1536, 256], P(None, 'wave', 'strip'), may hold values from -3 to 3
- psf_rows: bfloat16 [256, 4, 65], P('wave'), may hold values from -0.75 to 0.75
- psf_cols: bfloat16 [256, 4, 65], P('wave'), may hold values from -0.75 to 0.75
- pixel_mask: int32 [1536, 256], P('strip'), may hold values 0 or 1
- strip_lengths: int32 [16], P('strip'), may hold values from 32 to 96, as said below
Outputs:
- param_grad: float32 [9, 16, 24576], P(None, 'strip', 'wave')
Inputs may be any that keep to these rules, and one draw needn't show every extreme that they name: `strip_lengths`: the strip lengths sum to 1024; in every draw one strip holds 96 rows and one holds 32.
All inputs are finite; a program needn't handle non-finite values. No bound on the sum of `pixel_mask` on one device may be relied on, other than what follows from the above.
Results may differ from a plain program's by a relative error of at most 0.00098.
Values may be sent and summed in bfloat16 or wider, within the bound.
No kernel may reach another device: no remote copies, remote signals or barrier semaphores. Data moves between devices by JAX's collectives and lax.ppermute only.
A program may use at most 192 MiB of HBM per device.

v0:
```python
import jax
import jax.numpy as jnp
from jax import lax
from jax.sharding import PartitionSpec as P

parameter_low = (0.2, 0.4, 2.0, -0.8, 0.4, 0.3, 0.0, 0.0, 0.0)
parameter_span = (0.4, 0.6, 18.0, 1.6, 0.8, 1.2, 1.5, 3.141592653589793, 3.141592653589793)
stokes_weight = (1.0, 3.0, 3.0, 2.0)
loss_scale = 0.03125


def passed_along(shard, axis, by):
    count = lax.axis_size(axis)
    pairs = [(i, i + by) for i in range(count) if 0 <= i + by < count]
    return lax.ppermute(shard, axis, pairs)


def profile(distance, damping):
    scaled = distance / damping
    return 1.0 / (1.0 + scaled * scaled)


def stokes_model(unit_params, wave_grid):
    physical = [
        parameter_low[number] + parameter_span[number] * unit_params[number] for number in range(9)
    ]
    (
        source_zero,
        source_slope,
        strength,
        doppler,
        line_width,
        damping,
        zeeman_split,
        incline,
        azimuth,
    ) = physical
    offset = (wave_grid[:, None, None] - doppler) / line_width
    split_ratio = zeeman_split / line_width
    centre = profile(offset, damping)
    upper_line = profile(offset - split_ratio, damping)
    lower_line = profile(offset + split_ratio, damping)
    cosine = jnp.cos(incline)
    sine_value = jnp.sin(incline)
    sine_square = sine_value * sine_value
    absorb_total = 1.0 + strength * (
        centre * sine_square * 0.5 + (upper_line + lower_line) * (1.0 + cosine * cosine) * 0.25
    )
    linear = strength * (centre - 0.5 * (upper_line + lower_line)) * sine_square * 0.5
    linear_cosine = linear * jnp.cos(2.0 * azimuth)
    linear_sine = linear * jnp.sin(2.0 * azimuth)
    circular = strength * (lower_line - upper_line) * cosine * 0.5
    denominator = (
        absorb_total * absorb_total
        - linear_cosine * linear_cosine
        - linear_sine * linear_sine
        - circular * circular
    )
    source_ratio = source_slope / denominator
    return jnp.stack(
        [
            source_zero + source_ratio * absorb_total,
            -source_ratio * linear_cosine,
            -source_ratio * linear_sine,
            -source_ratio * circular,
        ]
    )


def band_tables(tap_table, out_rows, tap_count):
    in_rows = out_rows + tap_count - 1
    target_row = lax.broadcasted_iota(jnp.int32, (out_rows, in_rows, tap_count), 0)
    source_row = lax.broadcasted_iota(jnp.int32, (out_rows, in_rows, tap_count), 1)
    tap_index = lax.broadcasted_iota(jnp.int32, (out_rows, in_rows, tap_count), 2)
    selector = (source_row - target_row == tap_index).astype(jnp.bfloat16)
    return jnp.einsum(
        "wkt,ijt->wkij", tap_table, selector, preferred_element_type=jnp.float32
    ).astype(jnp.bfloat16)


def column_tables(tap_table, columns, tap_count):
    radius = tap_count // 2
    source_column = lax.broadcasted_iota(jnp.int32, (columns, columns, tap_count), 0)
    target_column = lax.broadcasted_iota(jnp.int32, (columns, columns, tap_count), 1)
    tap_index = lax.broadcasted_iota(jnp.int32, (columns, columns, tap_count), 2)
    selector = (source_column - target_column + radius == tap_index).astype(jnp.bfloat16)
    return jnp.einsum(
        "wkt,xyt->wkxy", tap_table, selector, preferred_element_type=jnp.float32
    ).astype(jnp.bfloat16)


def extend(upper_rim, middle, lower_rim, length, axis_index):
    radius = upper_rim.shape[axis_index]
    widened = jnp.concatenate([upper_rim, middle, jnp.zeros_like(upper_rim)], axis=axis_index)
    return lax.dynamic_update_slice_in_dim(widened, lower_rim, radius + length, axis_index)


def per_device(unit_params, observed, psf_rows, psf_cols, pixel_mask, strip_lengths):
    stokes_count, wave_count, capacity, columns = observed.shape
    tap_count = psf_rows.shape[2]
    radius = tap_count // 2
    gathered = lax.all_gather(unit_params, "wave", axis=2, tiled=True)
    own_params = gathered.reshape(gathered.shape[0], capacity, columns)
    length = strip_lengths[0]
    wave_pos = lax.axis_index("wave")
    levels = (wave_pos * wave_count + jnp.arange(wave_count, dtype=jnp.int32)).astype(jnp.float32)
    wave_grid = -3.0 + 6.0 * levels / (wave_count * lax.axis_size("wave") - 1)
    row_index = jnp.arange(capacity, dtype=jnp.int32)
    rows_live = (row_index < length).astype(jnp.float32)
    model_own = (stokes_model(own_params, wave_grid) * rows_live[:, None]).astype(jnp.bfloat16)
    tail_rows = lax.dynamic_slice_in_dim(model_own, length - radius, radius, 2)
    upper_rim = passed_along(tail_rows, "strip", 1)
    lower_rim = passed_along(model_own[:, :, :radius], "strip", -1)
    model_wide = extend(upper_rim, model_own, lower_rim, length, 2)
    row_band = band_tables(psf_rows, capacity, tap_count)
    column_band = column_tables(psf_cols, columns, tap_count)
    live_mask = pixel_mask.astype(jnp.float32) * rows_live[:, None]
    weight_square = jnp.array(stokes_weight, jnp.float32)
    weight_square = weight_square * weight_square
    block_size = 4
    block_count = wave_count // block_size

    def forward(number, residual_all):
        first_wave = number * block_size
        model_block = lax.dynamic_slice_in_dim(model_wide, first_wave, block_size, 1)
        band_block = lax.dynamic_slice_in_dim(row_band, first_wave, block_size, 0)
        column_block = lax.dynamic_slice_in_dim(column_band, first_wave, block_size, 0)
        observed_block = lax.dynamic_slice_in_dim(observed, first_wave, block_size, 1)
        row_pass = jnp.einsum(
            "wkij,swjc->kswic", band_block, model_block, preferred_element_type=jnp.float32
        ).astype(jnp.bfloat16)
        blurred = jnp.einsum(
            "kswic,wkcd->swid", row_pass, column_block, preferred_element_type=jnp.float32
        )
        residual = (
            loss_scale
            * weight_square[:, None, None, None]
            * live_mask
            * (blurred - observed_block.astype(jnp.float32))
        ).astype(jnp.bfloat16)
        return lax.dynamic_update_slice_in_dim(residual_all, residual, first_wave, 1)

    residual_all = lax.fori_loop(0, block_count, forward, jnp.zeros(observed.shape, jnp.bfloat16))
    row_back = band_tables(psf_rows[:, :, ::-1], capacity, tap_count)
    tail_residual = lax.dynamic_slice_in_dim(residual_all, length - radius, radius, 2)
    upper_resid = passed_along(tail_residual, "strip", 1)
    lower_resid = passed_along(residual_all[:, :, :radius], "strip", -1)
    residual_wide = extend(upper_resid, residual_all, lower_resid, length, 2)

    def backward(number, gradient_sum):
        first_wave = number * block_size
        residual_block = lax.dynamic_slice_in_dim(residual_wide, first_wave, block_size, 1)
        column_block = lax.dynamic_slice_in_dim(column_band, first_wave, block_size, 0)
        back_block = lax.dynamic_slice_in_dim(row_back, first_wave, block_size, 0)
        grid_block = lax.dynamic_slice_in_dim(wave_grid, first_wave, block_size, 0)
        across = jnp.einsum(
            "swjc,wkdc->kswjd", residual_block, column_block, preferred_element_type=jnp.float32
        ).astype(jnp.bfloat16)
        adjoint = (
            jnp.einsum("wkij,kswjc->swic", back_block, across, preferred_element_type=jnp.float32)
            * rows_live[:, None]
        )

        def model_of(params_now):
            return stokes_model(params_now, grid_block)

        unused_model, pullback = jax.vjp(model_of, own_params)
        return gradient_sum + pullback(adjoint)[0]

    gradient_local = lax.fori_loop(
        0, block_count, backward, jnp.zeros(own_params.shape, jnp.float32)
    )
    gradient_flat = gradient_local.reshape(gathered.shape)
    gradient_total = lax.psum(gradient_flat, "wave")
    share_width = unit_params.shape[2]
    return lax.dynamic_slice_in_dim(gradient_total, wave_pos * share_width, share_width, 2)


def solution(mesh):
    return jax.shard_map(
        per_device,
        mesh=mesh,
        in_specs=(
            P(None, "strip", "wave"),
            P(None, "wave", "strip", None),
            P("wave", None, None),
            P("wave", None, None),
            P("strip", None),
            P("strip"),
        ),
        out_specs=P(None, "strip", "wave"),
        check_vma=False,
    )
```

profile of v0, /device:TPU:0, one launch (start us, length us, event | category | flops | bytes accessed | tf_op | source)
XLA Modules:
  0.0 510.9 jit_solution(6636742498582574275)
XLA Ops:
  6.5 31.1 %all_gather.3 = f32[9,1,24576]{2,1,0:T(1,128)S(1)} all-gather(f32[9,1,3072]{2,1,0:T(1,128)} %param.11), channel_id=1, replica_groups=mesh['wave'=8,'strip'=16] {'wave'}, dimensions={2}, use_global_device_ids=true | all-gather | bytes 995328 | tf_op jit(solution)/shard_map/all_gather | solution.py:102
  37.6 9.9 %fusion.103 = (f32[24576]{0:T(1024)S(1)}, f32[24576]{0:T(1024)S(1)}, f32[24576]{0:T(1024)S(1)}, f32[24576]{0:T(1024)S(1)}, f32[24576]{0:T(1024)S(1)}, /*index=5*...) fusion(f32[9,1,24576]{2,1,0:T(1,128)S(1)} %all_gather.3), kind=kLoop, calls=%fused_computation.198 | loop fusion | flops 442368 | bytes 1966080 | tf_op jit(solution)/shard_map/add | solution.py:25
  48.7 5.3 %multiply_add_fusion.8 = (f32[1,32,96,256]{3,2,1,0:T(8,128)S(1)}, f32[1,32,96,256]{3,2,1,0:T(8,128)S(1)}, f32[1,32,96,256]{3,2,1,0:T(8,128)S(1)}, f32[1,32,96,256]{3,2,1,0:T(8,128)S(1)}) fusion(f32[96,256]{1,0:T(8,128)S(1)} %get-tuple-element.546, f32[96,256]{1,0:T(8,128)S(1)} %add.585, f32[96,256]{1,0:T(8,128)S(1)} %get-tuple-element.545, ...), kind=kLoop, calls=%fused_computation.166 | loop fusion | flops 37748736 | bytes 13860992 | tf_op jit(solution)/shard_map/add | solution.py:62
  54.0 2.0 fusion.74
  56.1 3.7 fusion.113
  60.0 2.6 collective-permute-start
  64.1 8.5 %convert_bitcast_fusion = bf16[32,4,256,256]{3,0,1,2:T(8,128)(2,1)} fusion(bf16[32,4,65]{2,1,0:T(4,128)(2,1)S(1)} %copy-done.4), kind=kOutput, calls=%fused_computation.149 | convolution fusion | flops 1111687168 | bytes 16793856 | tf_op jit(solution)/shard_map/wkt,xyt->wkxy/dot_general | solution.py:87
  72.6 16.3 %copy.20 = bf16[32,4,256,256]{3,2,1,0:T(8,128)(2,1)} copy(bf16[32,4,256,256]{3,0,1,2:T(8,128)(2,1)} %convert_bitcast_fusion) | data formatting | bytes 33554432
  89.0 3.9 convert_bitcast_fusion.2
  92.9 10.1 %maximum_maximum_fusion = bf16[4,32,160,256]{3,2,1,0:T(8,128)(2,1)} fusion(bf16[4,32,96,256]{3,2,1,0:T(8,128)(2,1)} %copy-done.1, bf16[4,32,32,256]{3,2,1,0:T(8,128)(2,1)} %collective-permute-done, bf16[160]{0:T(256)(128)(2,1)S(1)} %pad.113.clone), kind=kLoop, calls=%fused_computation.152 | loop fusion | flops 31457280 | bytes 18874688 | tf_op jit(solution)/shard_map/concatenate | solution.py:94
  103.0 20.4 %dynamic_update_slice.13 = bf16[4,32,160,256]{3,2,1,0:T(8,128)(2,1)} dynamic-update-slice(bf16[4,32,160,256]{3,2,1,0:T(8,128)(2,1)} %maximum_maximum_fusion, bf16[4,32,32,256]{3,2,1,0:T(8,128)(2,1)} %collective-permute-done.1, s32[]{:T(128)} %constant.278.clone.1, s32[]{:T(128)} %constant.278.clone.1, s32[]{:T(128)S(6)} %select_n.37, s32[]{:T(128)} %constant.278.clone.1) | dynamic-update-slice | bytes 4194308 | tf_op jit(solution)/shard_map/dynamic_update_slice | solution.py:95
  123.3 3.4 broadcast_in_dim.105.clone
  126.7 58.5 %while.31 = (s32[]{:T(128)}, bf16[4,32,96,256]{3,2,1,0:T(8,128)(2,1)}, f32[96,256]{1,0:T(8,128)S(1)}, bf16[32,4,256,256]{3,2,1,0:T(8,128)(2,1)}, bf16[4,32,160,2...) while((s32[]{:T(128)}, ...), condition=%wide.region_1.0_spmd.clone, body=%wide.region_0.0_spmd.clone.sunk | while | flops 1311866880 | bytes 9897691 | solution.py:143
  126.7 1.7 constant_dynamic-slice_fusion.11
  129.1 4.0 fusion.130
  136.4 4.0 fusion.130
  143.7 4.0 fusion.130
  151.0 4.0 fusion.130
  158.3 4.0 fusion.130
  165.6 4.0 fusion.130
  173.0 4.0 fusion.130
  180.3 4.0 fusion.130
  185.2 5.4 %fusion.112 = (bf16[4,32,32,256]{3,2,1,0:T(8,128)(2,1)}, bf16[4,32,32,256]{3,2,1,0:T(8,128)(2,1)}) fusion(bf16[4,32,96,256]{3,2,1,0:T(8,128)(2,1)} %get-tuple-element.364, s32[]{:T(128)S(6)} %select_n.36), kind=kLoop, calls=%fused_computation.217 | loop fusion | bytes 8388612 | tf_op jit(solution)/shard_map/slice | solution.py:147
  190.6 22.0 %collective-permute-start.2 = (bf16[4,32,32,256]{3,2,1,0:T(8,128)(2,1)}, bf16[4,32,32,256]{3,2,1,0:T(8,128)(2,1)}, u32[]{:S(2)}, u32[]{:S(2)}) collective-permute-start(bf16[4,32,32,256]{3,2,1,0:T(8,128)(2,1)} %get-tuple-element.537), channel_id=1, source_target_pairs={{0,1},{1,2},{2,3},{3,4},{4,5},{5,6},{6,7},{7,8},{8,9},{9,10},{10,1... | collective-permute-start | bytes 6291464 | tf_op jit(solution)/shard_map/ppermute | solution.py:15
  214.2 3.6 reduce.1
  217.8 1.9 copy.40
  219.7 4.0 convert_bitcast_fusion.1
  223.7 7.9 %maximum_maximum_fusion.1 = bf16[4,32,160,256]{3,2,1,0:T(8,128)(2,1)} fusion(bf16[4,32,96,256]{3,2,1,0:T(8,128)(2,1)S(1)} %copy-done, bf16[4,32,32,256]{3,2,1,0:T(8,128)(2,1)} %collective-permute-done.2, bf16[160]{0:T(256)(128)(2,1)S(1)} %pad.113.clone), kind=kLoop, calls=%fused_computation.153 | loop fusion | flops 31457280 | bytes 18874688 | tf_op jit(solution)/shard_map/concatenate | solution.py:94
  231.6 20.4 %dynamic_update_slice.14 = bf16[4,32,160,256]{3,2,1,0:T(8,128)(2,1)} dynamic-update-slice(bf16[4,32,160,256]{3,2,1,0:T(8,128)(2,1)} %maximum_maximum_fusion.1, bf16[4,32,32,256]{3,2,1,0:T(8,128)(2,1)} %collective-permute-done.3, s32[]{:T(128)} %constant.278.clone.1, s32[]{:T(128)} %constant.278.clone.1, s32[]{:T(128)S(6)} %select_n.37, s32[]{:T(128)} %constant.278.clone.1) | dynamic-update-slice | bytes 4194308 | tf_op jit(solution)/shard_map/dynamic_update_slice | solution.py:95
  252.0 134.8 %while.32 = (s32[]{:T(128)}, f32[9,96,256]{2,1,0:T(8,128)S(1)}, f32[9,96,256]{2,1,0:T(8,128)S(1)}, f32[32]{0:T(128)S(1)}, bf16[32,4,256,256]{3,2,1,0:T(8,128)(2,...) while((s32[]{:T(128)}, f32[9,96,256]{2,1,0:T(8,128)S(1)}, ...), condition=%wide.region_21.22_spmd.clone, body=%wide.region_2.21_spmd.clone.sunk | while | flops 1872642304 | bytes 34342920 | solution.py:170
  252.0 2.5 constant_dynamic-slice_fusion.12
  255.2 4.9 fusion.134
  268.8 2.5 constant_dynamic-slice_fusion.12
  272.0 4.9 fusion.134
  285.7 2.5 constant_dynamic-slice_fusion.12
  288.9 4.9 fusion.134
  302.5 2.5 constant_dynamic-slice_fusion.12
  305.7 4.9 fusion.134
  319.4 2.5 constant_dynamic-slice_fusion.12
  322.6 4.9 fusion.134
  336.2 2.5 constant_dynamic-slice_fusion.12
  339.4 4.9 fusion.134
  353.1 2.5 constant_dynamic-slice_fusion.12
  356.3 4.9 fusion.134
  369.9 2.5 constant_dynamic-slice_fusion.12
  373.1 4.9 fusion.134
  386.8 1.8 reshape.646
  388.6 113.9 %all-reduce.11.cloned.1.call-done = f32[9,1,24576]{2,1,0:T(1,128)} async-done(((f32[9,1,24576]{2,1,0:T(1,128)}), f32[9,1,24576]{2,1,0:T(1,128)}) %all-reduce.11.cloned.1.call-update) | async-done | bytes 884752 | tf_op jit(solution)/shard_map/psum | solution.py:174
  (192 shorter events, 105.3 us)
Async XLA Ops:
  6.5 496.0 %all-reduce.11.cloned.1.call-start = ((), (), s32[]{:S(2)}) async-start(), calls=%async_computation | async-start | bytes 1769472 | tf_op jit(solution)/shard_map/psum | solution.py:174
  56.1 3.9 copy-start.1
  56.1 8.0 %copy-start.4 = (bf16[32,4,65]{2,1,0:T(4,128)(2,1)S(1)}, bf16[32,4,65]{2,1,0:T(4,128)(2,1)}, u32[]{:S(2)}) copy-start(bf16[32,4,65]{2,1,0:T(4,128)(2,1)} %param.14) | copy-start | bytes 49924
  60.0 32.9 %collective-permute-start = (bf16[4,32,32,256]{3,2,1,0:T(8,128)(2,1)}, bf16[4,32,32,256]{3,2,1,0:T(8,128)(2,1)}, u32[]{:S(2)}, u32[]{:S(2)}) collective-permute-start(bf16[4,32,32,256]{3,2,1,0:T(8,128)(2,1)} %get-tuple-element.539), channel_id=1, source_target_pairs={{0,1},{1,2},{2,3},{3,4},{4,5},{5,6},{6,7},{7,8},{8,9},{9,10},{10,1... | collective-permute-start | bytes 6291464 | tf_op jit(solution)/shard_map/ppermute | solution.py:15
  62.6 40.3 %collective-permute-start.1 = (bf16[4,32,32,256]{3,2,1,0:T(8,128)(2,1)}, bf16[4,32,32,256]{3,2,1,0:T(8,128)(2,1)}, u32[]{:S(2)}, u32[]{:S(2)}) collective-permute-start(bf16[4,32,32,256]{3,2,1,0:T(8,128)(2,1)} %get-tuple-element.538), channel_id=1, source_target_pairs={{1,0},{2,1},{3,2},{4,3},{5,4},{6,5},{7,6},{8,7},{9,8},{10,9},{11,1... | collective-permute-start | bytes 6291464 | tf_op jit(solution)/shard_map/ppermute | solution.py:15
  72.6 16.4 %copy-start.3 = (s32[96,256]{1,0:T(8,128)S(1)}, s32[96,256]{1,0:T(8,128)}, u32[]{:S(2)}) copy-start(s32[96,256]{1,0:T(8,128)} %param.15) | copy-start | bytes 294916
  72.6 16.4 %copy-start.2 = (bf16[32,4,65]{2,1,0:T(4,128)(2,1)S(1)}, bf16[32,4,65]{2,1,0:T(4,128)(2,1)}, u32[]{:S(2)}) copy-start(bf16[32,4,65]{2,1,0:T(4,128)(2,1)} %param.13) | copy-start | bytes 49924
  123.3 3.4 copy-start.5
  190.6 33.1 %collective-permute-start.2 = (bf16[4,32,32,256]{3,2,1,0:T(8,128)(2,1)}, bf16[4,32,32,256]{3,2,1,0:T(8,128)(2,1)}, u32[]{:S(2)}, u32[]{:S(2)}) collective-permute-start(bf16[4,32,32,256]{3,2,1,0:T(8,128)(2,1)} %get-tuple-element.537), channel_id=1, source_target_pairs={{0,1},{1,2},{2,3},{3,4},{4,5},{5,6},{6,7},{7,8},{8,9},{9,10},{10,1... | collective-permute-start | bytes 6291464 | tf_op jit(solution)/shard_map/ppermute | solution.py:15
  212.6 19.0 %collective-permute-start.3 = (bf16[4,32,32,256]{3,2,1,0:T(8,128)(2,1)}, bf16[4,32,32,256]{3,2,1,0:T(8,128)(2,1)}, u32[]{:S(2)}, u32[]{:S(2)}) collective-permute-start(bf16[4,32,32,256]{3,2,1,0:T(8,128)(2,1)} %get-tuple-element.536), channel_id=1, source_target_pairs={{1,0},{2,1},{3,2},{4,3},{5,4},{6,5},{7,6},{8,7},{9,8},{10,9},{11,1... | collective-permute-start | bytes 6291464 | tf_op jit(solution)/shard_map/ppermute | solution.py:15
  219.7 4.0 copy-start
Sparse Core Ops, SparseCore 0:
  388.8 113.6 all-reduce.10
where the time goes:
time: 514 us; the launch traced here: 511 us
  local copies, waits for them, and re-layouts  122 us (24%)
  other arithmetic  114 us (22%)
  waiting for transfers between devices  114 us (22%)
  matrix products  87 us (17%)
  blocking collectives  31.1 us (6%)
  starting transfers between devices  27.5 us (5%)
  between operations  14.3 us (3%)
    psum x1, waiting for transfers between devices, per_device(): gradient_total = lax.psum(gradient_flat, 'wave')  114 us
    dynamic_update_slice x2, local copies, waits for them, and re-layouts, extend(): lax.dynamic_update_slice_in_dim(widened, lower_rim, radius + length, axis...  40.8 us
    dot_general x8, matrix products, backward(): jnp.einsum('wkij,kswjc->swic', back_block, across, preferred_element_type...  39.1 us
    dot_general x8, matrix products, forward(): jnp.einsum('kswic,wkcd->swid', row_pass, column_block, preferred_element_...  31.6 us
    all_gather x1, blocking collectives, per_device(): gathered = lax.all_gather(unit_params, 'wave', axis=2, tiled=True)  31.1 us
    ppermute x4, starting transfers between devices, passed_along(): return lax.ppermute(shard, axis, pairs)  27.5 us
    mul x32, other arithmetic, stokes_model(): parameter_span[number] * unit_params[number]  22.7 us
    dynamic_slice x8, local copies, waits for them, and re-layouts, backward(): back_block = lax.dynamic_slice_in_dim(row_back, first_wave, block_size, 0)  20.2 us
  transfers between devices with their start and end apart: 5, of which 1 were waited for; matrix products, arithmetic and copies ran while one was open for 11% of the time, Pallas kernels for 0%

commit v1 on v0

--- a/solution.py
+++ b/solution.py
@@ -99,7 +99,9 @@
     stokes_count, wave_count, capacity, columns = observed.shape
     tap_count = psf_rows.shape[2]
     radius = tap_count // 2
-    gathered = lax.all_gather(unit_params, "wave", axis=2, tiled=True)
+    gathered = jnp.concatenate(
+        lax.all_to_all(jnp.stack([unit_params] * lax.axis_size("wave")), "wave", 0, 0), axis=2
+    )
     own_params = gathered.reshape(gathered.shape[0], capacity, columns)
     length = strip_lengths[0]
     wave_pos = lax.axis_index("wave")

time: 514 us -> 499 us (0.971)
  blocking collectives: 31.1 us -> 0 us
  waiting for transfers between devices: 114 us -> 131 us
  local copies, waits for them, and re-layouts: 122 us -> 110 us
  matrix products: 87 us -> 94.7 us
  starting transfers between devices: 27.5 us -> 33.1 us
    all_gather x1 -> x0, blocking collectives: 31.1 us -> none  [per_device(): gathered = lax.all_gather(unit_params, 'wave', axis=2, tiled=True)]
    all_to_all x0 -> x1, waiting for transfers between devices: none -> 13.2 us  [per_device(): lax.all_to_all(jnp.stack([unit_params] * lax.axis_size('wave')), 'wave',...]
    dot_general x8, matrix products: 31.6 us -> 39.4 us  [forward(): jnp.einsum('kswic,wkcd->swid', row_pass, column_block, preferred_element_...]
    dynamic_update_slice x8 -> x0, local copies, waits for them, and re-layouts: 7.64 us -> none  [forward(): lax.dynamic_update_slice_in_dim(residual_all, residual, first_wave, 1)]
    all_to_all x0 -> x1, starting transfers between devices: none -> 5.77 us  [per_device(): lax.all_to_all(jnp.stack([unit_params] * lax.axis_size('wave')), 'wave',...]
    dynamic_slice x16 -> x8, local copies, waits for them, and re-layouts: 18.2 us -> 13.3 us  [forward(): band_block = lax.dynamic_slice_in_dim(row_band, first_wave, block_size, 0)]
    unnamed x14 -> x12, local copies, waits for them, and re-layouts: 18.4 us -> 17.5 us
  transfers between devices with their start and end apart: 5 -> 6, of which waited for: 1 -> 2; matrix products, arithmetic and copies ran while one was open for 11% -> 11% of each run, Pallas kernels for 0% -> 0%
where the time goes in v1:
time: 499 us; the launch traced here: 495 us
  waiting for transfers between devices  131 us (26%)
  other arithmetic  112 us (22%)
  local copies, waits for them, and re-layouts  110 us (22%)
  matrix products  94.7 us (19%)
  starting transfers between devices  33.1 us (7%)
  between operations  14.3 us (3%)
    psum x1, waiting for transfers between devices, per_device(): gradient_total = lax.psum(gradient_flat, 'wave')  117 us
    dynamic_update_slice x2, local copies, waits for them, and re-layouts, extend(): lax.dynamic_update_slice_in_dim(widened, lower_rim, radius + length, axis...  40.4 us
    dot_general x8, matrix products, forward(): jnp.einsum('kswic,wkcd->swid', row_pass, column_block, preferred_element_...  39.4 us
    dot_general x8, matrix products, backward(): jnp.einsum('wkij,kswjc->swic', back_block, across, preferred_element_type...  39 us
    ppermute x4, starting transfers between devices, passed_along(): return lax.ppermute(shard, axis, pairs)  27.3 us
    mul x32, other arithmetic, stokes_model(): parameter_span[number] * unit_params[number]  22.7 us
    concatenate x2, other arithmetic, extend(): jnp.concatenate([upper_rim, middle, jnp.zeros_like(upper_rim)], axis=axis...  20.4 us
    dynamic_slice x8, local copies, waits for them, and re-layouts, backward(): back_block = lax.dynamic_slice_in_dim(row_back, first_wave, block_size, 0)  20.2 us
  transfers between devices with their start and end apart: 6, of which 2 were waited for; matrix products, arithmetic and copies ran while one was open for 11% of the time, Pallas kernels for 0%

profile of v1, /device:TPU:0, one launch (start us, length us, event | category | flops | bytes accessed | tf_op | source)
XLA Modules:
  0.0 495.4 jit_solution(8865947715357919205)
XLA Ops:
  8.8 5.8 %all-to-all-start = ((f32[8,9,1,3072]{3,2,1,0:T(1,128)}), f32[8,9,1,3072]{3,2,1,0:T(1,128)S(1)}, u32[]{:S(2)}, u32[]{:S(2)}) async-start(f32[8,9,1,3072]{3,2,1,0:T(1,128)} %stack.4), calls=%async_computation | async-start | bytes 1769472 | tf_op jit(solution)/shard_map/all_to_all | solution.py:103
  15.3 13.2 %all-to-all-done = f32[8,9,1,3072]{3,2,1,0:T(1,128)S(1)} async-done(((f32[8,9,1,3072]{3,2,1,0:T(1,128)}), f32[8,9,1,3072]{3,2,1,0:T(1,128)S(1)}, u32[]{:S(2)}, u32[]{:S(2)}) %all-to-all-start) | async-done | bytes 884768 | tf_op jit(solution)/shard_map/all_to_all | solution.py:103
  28.6 8.7 %fusion.111 = (f32[8,3072]{1,0:T(8,128)S(1)}, f32[8,3072]{1,0:T(8,128)S(1)}, f32[8,3072]{1,0:T(8,128)S(1)}, f32[8,3072]{1,0:T(8,128)S(1)}, f32[8,3072]{1,0:T(8,1...) fusion(f32[9,1,8,3072]{3,1,0,2:T(1,128)S(1)} %bitcast.276), kind=kLoop, calls=%fused_computation.199 | loop fusion | flops 442368 | bytes 1966080 | tf_op jit(solution)/shard_map/add | solution.py:25
  37.7 5.3 %multiply_add_fusion.8 = (f32[1,32,96,256]{3,2,0,1:T(8,128)S(1)}, f32[1,32,96,256]{3,2,0,1:T(8,128)S(1)}, f32[1,32,96,256]{3,2,0,1:T(8,128)S(1)}, f32[1,32,96,256]{3,2,0,1:T(8,128)S(1)}) fusion(f32[96,256]{1,0:T(8,128)S(1)} %get-tuple-element.591, f32[96,256]{1,0:T(8,128)S(1)} %add.585, f32[96,256]{1,0:T(8,128)S(1)} %get-tuple-element.590, ...), kind=kLoop, calls=%fused_computation.166 | loop fusion | flops 37748736 | bytes 13860992 | tf_op jit(solution)/shard_map/add | solution.py:62
  43.0 2.1 fusion.82
  45.2 3.7 fusion.121
  49.1 2.9 collective-permute-start
  53.5 8.5 %convert_bitcast_fusion = bf16[32,4,256,256]{3,0,1,2:T(8,128)(2,1)} fusion(bf16[32,4,65]{2,1,0:T(4,128)(2,1)S(1)} %copy-done.3), kind=kOutput, calls=%fused_computation.149 | convolution fusion | flops 1111687168 | bytes 16793856 | tf_op jit(solution)/shard_map/wkt,xyt->wkxy/dot_general | solution.py:87
  62.0 16.3 %copy.58 = bf16[32,4,256,256]{3,2,1,0:T(8,128)(2,1)} copy(bf16[32,4,256,256]{3,0,1,2:T(8,128)(2,1)} %convert_bitcast_fusion) | data formatting | bytes 33554432
  78.4 3.9 convert_bitcast_fusion.2
  82.3 10.1 %maximum_maximum_fusion = bf16[4,32,160,256]{3,2,0,1:T(8,128)(2,1)} fusion(bf16[4,32,96,256]{3,2,0,1:T(8,128)(2,1)} %copy-done, bf16[4,32,32,256]{3,2,0,1:T(8,128)(2,1)} %collective-permute-done, bf16[160]{0:T(256)(128)(2,1)S(1)} %pad.113.clone), kind=kLoop, calls=%fused_computation.152 | loop fusion | flops 31457280 | bytes 18874688 | tf_op jit(solution)/shard_map/concatenate | solution.py:94
  92.4 20.2 %dynamic_update_slice.13 = bf16[4,32,160,256]{3,2,0,1:T(8,128)(2,1)} dynamic-update-slice(bf16[4,32,160,256]{3,2,0,1:T(8,128)(2,1)} %maximum_maximum_fusion, bf16[4,32,32,256]{3,2,0,1:T(8,128)(2,1)} %collective-permute-done.1, s32[]{:T(128)} %constant.278.clone.1, s32[]{:T(128)} %constant.278.clone.1, s32[]{:T(128)S(6)} %select_n.37, s32[]{:T(128)} %constant.278.clone.1) | dynamic-update-slice | bytes 4194308 | tf_op jit(solution)/shard_map/dynamic_update_slice | solution.py:95
  112.6 3.4 broadcast_in_dim.105
  116.0 53.5 %while.31 = (s32[]{:T(128)}, bf16[4,32,96,256]{3,2,0,1:T(8,128)(2,1)}, f32[96,256]{1,0:T(8,128)S(1)}, bf16[32,4,256,256]{3,2,1,0:T(8,128)(2,1)}, bf16[4,32,160,2...) while((s32[]{:T(128)}, ...), condition=%wide.region_1.0_spmd.clone, body=%wide.region_0.0_spmd.clone.sunk | while | flops 1311866880 | bytes 7342295 | solution.py:145
  116.0 1.7 constant_dynamic-slice_fusion.11
  117.7 4.9 fusion.136
  122.6 1.7 constant_dynamic-slice_fusion.11
  124.4 4.9 fusion.136
  131.1 4.9 fusion.136
  137.7 5.0 %fusion.136 = bf16[4,32,96,256]{3,2,0,1:T(8,128)(2,1)} fusion(bf16[4,32,96,256]{3,2,0,1:T(8,128)(2,1)} %get-tuple-element.809, s32[]{:T(128)S(6)} %select_n.43, bf16[32,4,256,256]{3,2,1,0:T(8,128)(2,1)} %get-tuple-element.823, bf16[4,32,160,256]{3,2,0,1:T(8,128)(2,1)} %get-tuple-element.824, f32[4,96,256]{2,1,0:T(8,128)S(1)} %broadcast_multiply_fusion.11, ...), kind=kOutput, calls=%fused_computation.11.clone.1 | convolution fusion | flops 1311768576 | bytes 5867520 | tf_op jit(solution)/shard_map/while/body/eval_jaxpr/kswic,wkcd->swid/dot_general | solution.py:134
  144.5 4.9 fusion.136
  151.2 4.9 fusion.136
  157.9 4.9 fusion.136
  164.6 4.9 fusion.136
  169.5 5.5 %fusion.120 = (bf16[4,32,32,256]{3,2,0,1:T(8,128)(2,1)}, bf16[4,32,32,256]{3,2,0,1:T(8,128)(2,1)}) fusion(bf16[4,32,96,256]{3,2,0,1:T(8,128)(2,1)} %get-tuple-element.364, s32[]{:T(128)S(6)} %select_n.36), kind=kLoop, calls=%fused_computation.218 | loop fusion | bytes 8388612 | tf_op jit(solution)/shard_map/slice | solution.py:149
  175.0 21.7 %collective-permute-start.2 = (bf16[4,32,32,256]{3,2,0,1:T(8,128)(2,1)}, bf16[4,32,32,256]{3,2,0,1:T(8,128)(2,1)}, u32[]{:S(2)}, u32[]{:S(2)}) collective-permute-start(bf16[4,32,32,256]{3,2,0,1:T(8,128)(2,1)} %get-tuple-element.582), channel_id=1, source_target_pairs={{0,1},{1,2},{2,3},{3,4},{4,5},{5,6},{6,7},{7,8},{8,9},{9,10},{10,1... | collective-permute-start | bytes 6291464 | tf_op jit(solution)/shard_map/ppermute | solution.py:15
  198.1 4.0 convert_bitcast_fusion.1
  202.4 10.3 %maximum_maximum_fusion.1 = bf16[4,32,160,256]{3,2,0,1:T(8,128)(2,1)} fusion(bf16[4,32,96,256]{3,2,0,1:T(8,128)(2,1)} %get-tuple-element.364, bf16[4,32,32,256]{3,2,0,1:T(8,128)(2,1)} %collective-permute-done.2, bf16[160]{0:T(256)(128)(2,1)S(1)} %pad.113.clone), kind=kLoop, calls=%fused_computation.153 | loop fusion | flops 31457280 | bytes 18874688 | tf_op jit(solution)/shard_map/concatenate | solution.py:94
  212.8 20.2 %dynamic_update_slice.14 = bf16[4,32,160,256]{3,2,0,1:T(8,128)(2,1)} dynamic-update-slice(bf16[4,32,160,256]{3,2,0,1:T(8,128)(2,1)} %maximum_maximum_fusion.1, bf16[4,32,32,256]{3,2,0,1:T(8,128)(2,1)} %collective-permute-done.3, s32[]{:T(128)} %constant.278.clone.1, s32[]{:T(128)} %constant.278.clone.1, s32[]{:T(128)S(6)} %select_n.37, s32[]{:T(128)} %constant.278.clone.1) | dynamic-update-slice | bytes 4194308 | tf_op jit(solution)/shard_map/dynamic_update_slice | solution.py:95
  233.0 134.8 %while.32 = (s32[]{:T(128)}, f32[9,96,256]{2,1,0:T(8,128)S(1)}, f32[9,96,256]{2,1,0:T(8,128)S(1)}, f32[32]{0:T(128)S(1)}, bf16[32,4,256,256]{3,2,1,0:T(8,128)(2,...) while((s32[]{:T(128)}, f32[9,96,256]{2,1,0:T(8,128)S(1)}, ...), condition=%wide.region_21.22_spmd.clone, body=%wide.region_2.21_spmd.clone.sunk | while | flops 1872642304 | bytes 34342920 | solution.py:172
  233.0 2.5 constant_dynamic-slice_fusion.12
  236.2 4.9 fusion.140
  249.8 2.5 constant_dynamic-slice_fusion.12
  253.0 4.9 fusion.140
  266.7 2.5 constant_dynamic-slice_fusion.12
  269.9 4.9 fusion.140
  283.5 2.5 constant_dynamic-slice_fusion.12
  286.7 4.9 fusion.140
  300.4 2.5 constant_dynamic-slice_fusion.12
  303.6 4.9 fusion.140
  317.2 2.5 constant_dynamic-slice_fusion.12
  320.4 4.9 fusion.140
  334.1 2.5 constant_dynamic-slice_fusion.12
  337.3 4.9 fusion.140
  350.9 2.5 constant_dynamic-slice_fusion.12
  354.1 4.9 fusion.140
  367.8 1.8 reshape.649
  369.6 117.4 %all-reduce.11.cloned.1.call-done = f32[9,1,24576]{2,1,0:T(1,128)} async-done(((f32[9,1,24576]{2,1,0:T(1,128)}), f32[9,1,24576]{2,1,0:T(1,128)}) %all-reduce.11.cloned.1.call-update) | async-done | bytes 884752 | tf_op jit(solution)/shard_map/psum | solution.py:176
  (176 shorter events, 93.5 us)
Async XLA Ops:
  8.8 19.7 %all-to-all-start = ((f32[8,9,1,3072]{3,2,1,0:T(1,128)}), f32[8,9,1,3072]{3,2,1,0:T(1,128)S(1)}, u32[]{:S(2)}, u32[]{:S(2)}) async-start(f32[8,9,1,3072]{3,2,1,0:T(1,128)} %stack.4), calls=%async_computation | async-start | bytes 1769472 | tf_op jit(solution)/shard_map/all_to_all | solution.py:103
  14.6 472.4 %all-reduce.11.cloned.1.call-start = ((), (), s32[]{:S(2)}) async-start(), calls=%async_computation.1 | async-start | bytes 1769472 | tf_op jit(solution)/shard_map/psum | solution.py:176
  45.1 3.9 copy-start
  45.2 8.3 %copy-start.3 = (bf16[32,4,65]{2,1,0:T(4,128)(2,1)S(1)}, bf16[32,4,65]{2,1,0:T(4,128)(2,1)}, u32[]{:S(2)}) copy-start(bf16[32,4,65]{2,1,0:T(4,128)(2,1)} %param.14) | copy-start | bytes 49924
  49.1 33.2 %collective-permute-start = (bf16[4,32,32,256]{3,2,0,1:T(8,128)(2,1)}, bf16[4,32,32,256]{3,2,0,1:T(8,128)(2,1)}, u32[]{:S(2)}, u32[]{:S(2)}) collective-permute-start(bf16[4,32,32,256]{3,2,0,1:T(8,128)(2,1)} %get-tuple-element.584), channel_id=1, source_target_pairs={{0,1},{1,2},{2,3},{3,4},{4,5},{5,6},{6,7},{7,8},{8,9},{9,10},{10,1... | collective-permute-start | bytes 6291464 | tf_op jit(solution)/shard_map/ppermute | solution.py:15
  52.0 40.4 %collective-permute-start.1 = (bf16[4,32,32,256]{3,2,0,1:T(8,128)(2,1)}, bf16[4,32,32,256]{3,2,0,1:T(8,128)(2,1)}, u32[]{:S(2)}, u32[]{:S(2)}) collective-permute-start(bf16[4,32,32,256]{3,2,0,1:T(8,128)(2,1)} %get-tuple-element.583), channel_id=1, source_target_pairs={{1,0},{2,1},{3,2},{4,3},{5,4},{6,5},{7,6},{8,7},{9,8},{10,9},{11,1... | collective-permute-start | bytes 6291464 | tf_op jit(solution)/shard_map/ppermute | solution.py:15
  62.0 16.4 %copy-start.2 = (s32[96,256]{1,0:T(8,128)S(1)}, s32[96,256]{1,0:T(8,128)}, u32[]{:S(2)}) copy-start(s32[96,256]{1,0:T(8,128)} %param.15) | copy-start | bytes 294916
  62.0 16.4 %copy-start.1 = (bf16[32,4,65]{2,1,0:T(4,128)(2,1)S(1)}, bf16[32,4,65]{2,1,0:T(4,128)(2,1)}, u32[]{:S(2)}) copy-start(bf16[32,4,65]{2,1,0:T(4,128)(2,1)} %param.13) | copy-start | bytes 49924
  112.6 3.4 copy-start.4
  175.0 27.5 %collective-permute-start.2 = (bf16[4,32,32,256]{3,2,0,1:T(8,128)(2,1)}, bf16[4,32,32,256]{3,2,0,1:T(8,128)(2,1)}, u32[]{:S(2)}, u32[]{:S(2)}) collective-permute-start(bf16[4,32,32,256]{3,2,0,1:T(8,128)(2,1)} %get-tuple-element.582), channel_id=1, source_target_pairs={{0,1},{1,2},{2,3},{3,4},{4,5},{5,6},{6,7},{7,8},{8,9},{9,10},{10,1... | collective-permute-start | bytes 6291464 | tf_op jit(solution)/shard_map/ppermute | solution.py:15
  196.6 16.2 %collective-permute-start.3 = (bf16[4,32,32,256]{3,2,0,1:T(8,128)(2,1)}, bf16[4,32,32,256]{3,2,0,1:T(8,128)(2,1)}, u32[]{:S(2)}, u32[]{:S(2)}) collective-permute-start(bf16[4,32,32,256]{3,2,0,1:T(8,128)(2,1)} %get-tuple-element.581), channel_id=1, source_target_pairs={{1,0},{2,1},{3,2},{4,3},{5,4},{6,5},{7,6},{8,7},{9,8},{10,9},{11,1... | collective-permute-start | bytes 6291464 | tf_op jit(solution)/shard_map/ppermute | solution.py:15
Sparse Core Ops, SparseCore 0:
  369.7 117.2 all-reduce.10
